TPU v7x, 32 devices: a whole 2x2x4 slice. The times are simulated.
32 devices in a mesh: ctx: 8 (over y, x, core), mp: 4 (over z).
Axes of the slice: x: 2, y: 2, z: 4, core: 2. Of those that a mesh axis runs over, the one named last changes fastest.
Arguments:
- cotangent: bfloat16 [1536, 8192], P('ctx', 'mp'), may hold values from -6 to 6
- out_weight: bfloat16 [8192, 8192], P('mp', 'ctx'), may hold values from -0.0625 to 0.0625
- query_act: bfloat16 [1536, 8192], P('ctx', 'mp'), may hold values from -6 to 6
- key_act: bfloat16 [1536, 8192], P('ctx', 'mp'), may hold values from -6 to 6
- value_act: bfloat16 [1536, 8192], P('ctx', 'mp'), may hold values from -6 to 6
- filters: float32 [512, 128], replicated, may hold values from -0.5 to 0.5
Outputs:
- grad_query: bfloat16 [1536, 8192], P('ctx', 'mp')
- grad_key: bfloat16 [1536, 8192], P('ctx', 'mp')
- grad_value: bfloat16 [1536, 8192], P('ctx', 'mp')
- grad_filters: float32 [512, 128], replicated
All inputs are finite; a program needn't handle non-finite values.
Results may differ from a plain program's by a relative error of at most 0.0051.
Values may be sent and summed in bfloat16 or wider, within the bound.
No kernel may reach another device: no remote copies, remote signals or barrier semaphores. Data moves between devices by JAX's collectives and lax.ppermute only.
A program may use at most 128 MiB of HBM per device.

v0:
```python
import jax
import jax.numpy as jnp
from jax import lax
from jax.sharding import PartitionSpec as P


def causal(widened, taps, rows, prev):

    def causal_step(shift, total):
        window = lax.dynamic_slice_in_dim(widened, (prev - shift).astype(jnp.int32), rows, 0)
        weight = lax.dynamic_slice_in_dim(taps, shift.astype(jnp.int32), 1, 0)
        return total + weight * window

    return lax.fori_loop(
        jnp.int32(0),
        jnp.int32(prev + 1),
        causal_step,
        jnp.zeros((rows, widened.shape[1]), widened.dtype),
    )


def anticausal(trailing, taps, rows, prev):

    def anticausal_step(shift, total):
        window = lax.dynamic_slice_in_dim(trailing, shift.astype(jnp.int32), rows, 0)
        weight = lax.dynamic_slice_in_dim(taps, shift.astype(jnp.int32), 1, 0)
        return total + weight * window

    return lax.fori_loop(
        jnp.int32(0),
        jnp.int32(prev + 1),
        anticausal_step,
        jnp.zeros((rows, trailing.shape[1]), trailing.dtype),
    )


def lagged(widened, gradient, prev):
    rows = gradient.shape[0]

    def one_lag(shift):
        window = lax.dynamic_slice_in_dim(widened, prev - shift, rows, 0)
        return jnp.sum(window * gradient, axis=0)

    return lax.map(one_lag, jnp.arange(prev + 1, dtype=jnp.int32))


def contract(left, right):
    return lax.dot_general(
        left, right, (((1,), (1,)), ((), ())), preferred_element_type=jnp.float32
    )


def group_table(first, count, per_group, groups):
    channel = first + jnp.arange(count)
    return (channel[None, :] // per_group == jnp.arange(groups)[:, None]).astype(jnp.float32)


def body(cotangent, out_weight, query_act, key_act, value_act, filters):
    tok_rows, chans = cotangent.shape
    groups, taps_len = filters.shape
    prev = taps_len - 1
    ctx_count = lax.axis_size("ctx")
    per_group = chans * lax.axis_size("mp") // groups
    panel = lax.all_gather(out_weight, "ctx", axis=1, tiled=True)
    grad_mixed = contract(lax.all_gather(cotangent, "mp", axis=1, tiled=True), panel)
    product = (key_act.astype(jnp.float32) * value_act.astype(jnp.float32)).astype(jnp.bfloat16)
    grad_conv = (grad_mixed * query_act.astype(jnp.float32)).astype(jnp.bfloat16)
    narrow = chans // ctx_count
    seq_product, seq_grad = (
        lax.all_to_all(product, "ctx", split_axis=1, concat_axis=0, tiled=True),
        lax.all_to_all(grad_conv, "ctx", split_axis=1, concat_axis=0, tiled=True),
    )
    onehot = group_table(
        lax.axis_index("mp") * chans + lax.axis_index("ctx") * narrow, narrow, per_group, groups
    )
    taps = jnp.dot(filters.T, onehot, precision=lax.Precision.HIGHEST)
    seq_rows = seq_grad.shape[0]
    grad_wide = seq_grad.astype(jnp.float32)
    widened = jnp.concatenate(
        [jnp.zeros((prev, narrow), jnp.float32), seq_product.astype(jnp.float32)], 0
    )
    trailing = jnp.concatenate([grad_wide, jnp.zeros((prev, narrow), jnp.float32)], 0)
    seq_mixed = causal(widened, taps, seq_rows, prev)
    seq_back = anticausal(trailing, taps, seq_rows, prev)
    corr = lagged(widened, grad_wide, prev)
    mixed, grad_product = (
        lax.all_to_all(seq_mixed, "ctx", split_axis=0, concat_axis=1, tiled=True),
        lax.all_to_all(seq_back, "ctx", split_axis=0, concat_axis=1, tiled=True),
    )
    grad_query = (grad_mixed * mixed).astype(jnp.bfloat16)
    grad_key = (grad_product * value_act.astype(jnp.float32)).astype(jnp.bfloat16)
    grad_value = (grad_product * key_act.astype(jnp.float32)).astype(jnp.bfloat16)
    partial_terms = jnp.dot(onehot, corr.T, precision=lax.Precision.HIGHEST)
    scale = (tok_rows * ctx_count * per_group) ** (-0.5)
    grad_filters = lax.psum(partial_terms, ("ctx", "mp")) * scale
    return (grad_query, grad_key, grad_value, grad_filters)


def solution(mesh):
    in_specs = (P("ctx", "mp"), P("mp", "ctx"), P("ctx", "mp"), P("ctx", "mp"), P("ctx", "mp"), P())
    out_specs = (P("ctx", "mp"), P("ctx", "mp"), P("ctx", "mp"), P())
    return jax.shard_map(body, mesh=mesh, in_specs=in_specs, out_specs=out_specs, check_vma=False)
```

profile of v0, /device:TPU:0, one launch (start us, length us, event | category | flops | bytes accessed | tf_op | source)
XLA Modules:
  0.0 1397.0 jit_solution(9679557478164837878)
XLA Ops:
  8.7 67.1 %all-gather.3.cloned.1.call-done = bf16[192,8192]{1,0:T(8,128)(2,1)} async-done(((bf16[192,2048]{1,0:T(8,128)(2,1)}), bf16[192,8192]{1,0:T(8,128)(2,1)}) %all-gather.3.cloned.1.call-update) | async-done | bytes 3145744 | tf_op jit(solution)/shard_map/all_gather | solution.py:65
  75.8 161.4 %all-gather.5.cloned.1.call-done = bf16[2048,8192]{1,0:T(8,128)(2,1)} async-done(((bf16[2048,1024]{1,0:T(8,128)(2,1)}), bf16[2048,8192]{1,0:T(8,128)(2,1)}) %all-gather.5.cloned.1.call-update) | async-done | bytes 33554448 | tf_op jit(solution)/shard_map/all_gather | solution.py:64
  237.2 18.0 %multiply_convert_fusion = (bf16[192,2048]{1,0:T(8,128)(2,1)S(1)}, f32[192,2048]{1,0:T(8,128)}) fusion(bf16[192,2048]{1,0:T(8,128)(2,1)S(1)} %copy-done.7, bf16[192,8192]{1,0:T(8,128)(2,1)} %all-gather.3.cloned.1.call-done, bf16[2048,8192]{1,0:T(8,128)(2,1)} %all-gather.5.cloned.1.call-done), kind=kOutput, calls=%fused_computation.11 | convolution fusion | flops 6443630592 | bytes 39845888 | tf_op jit(solution)/shard_map/dot_general | solution.py:48
  256.1 3.5 all-to-all-start.2
  260.5 11.8 all-to-all-done.2
  274.4 282.6 %while.38 = (s32[]{:T(128)}, f32[1536,256]{1,0:T(8,128)S(1)}, f32[128,256]{1,0:T(8,128)S(1)}, f32[1663,256]{1,0:T(8,128)}, s32[]{:T(128)}, /*index=5*/s32[]{:T(128)}) while((s32[]{:T(128)}, f32[1536,256]{1,0:T(8,128)S(1)}, f32[128,256]{1,0:T(8,128)S(1)}, f32[1663,256]{1,0:T(8,128)}, s32[]{:T(128)}, /*index=5*/s32[]{:T(128)}) %tuple.98), condition=%wide.region_3.4_spmd.clone, body=%wide.region_2.3_spmd.clone.sunk | while | flops 1179651 | bytes 4721759 | solution.py:29
  557.0 23.4 %all_to_all.64 = f32[8,192,256]{2,1,0:T(8,128)S(1)} all-to-all(f32[8,192,256]{2,1,0:T(8,128)S(1)} %bitcast.45), channel_id=1, replica_groups=mesh['ctx'=8,'mp'=4] {'ctx'}, dimensions={0} | all-to-all | bytes 3145728 | tf_op jit(solution)/shard_map/all_to_all | solution.py:88
  584.3 3.5 all-to-all-start
  587.9 12.5 all-to-all-done
  602.6 364.1 %while.37 = (s32[]{:T(128)}, f32[1536,256]{1,0:T(8,128)}, f32[128,256]{1,0:T(8,128)S(1)}, f32[1663,256]{1,0:T(8,128)S(1)}, s32[]{:T(128)}, /*index=5*/s32[]{:T(128)}, s32[]{:T(128)}, s32[]{:T(128)}) while((s32[]{:T(128)}, f32[1536,256]{1,0:T(8,128)}, f32[128,256]{1,0:T(8,128)S(1)}, f32[1663,256]{1,0:T(8,128)S(1)}, s32[]{:T(128)}, ...), condition=%wide.region_1.2_spmd.clone, body=%wide.region_0.1_spmd.clone.sunk | while | flops 1179655 | bytes 4721821 | solution.py:14
  607.0 2.9 select_add_fusion.4
  609.9 2.9 select_add_fusion.4
  618.6 2.9 select_add_fusion.4
  621.5 2.9 select_add_fusion.4
  646.9 2.9 select_add_fusion.4
  652.7 2.9 select_add_fusion.4
  655.6 2.9 select_add_fusion.4
  664.3 2.9 select_add_fusion.4
  667.2 2.9 select_add_fusion.4
  692.6 2.9 select_add_fusion.4
  698.4 2.9 select_add_fusion.4
  701.3 2.9 select_add_fusion.4
  710.0 2.9 select_add_fusion.4
  712.9 2.9 select_add_fusion.4
  738.3 2.9 select_add_fusion.4
  744.1 2.9 select_add_fusion.4
  747.0 2.9 select_add_fusion.4
  755.6 2.9 select_add_fusion.4
  758.5 2.9 select_add_fusion.4
  966.7 4.3 all-to-all-start.1
  971.0 287.3 %while.36 = (s32[]{:T(128)}, f32[128,256]{1,0:T(8,128)S(1)}, s32[128]{0:T(128)S(1)}, f32[1663,256]{1,0:T(8,128)S(1)}, f32[1536,256]{1,0:T(8,128)S(1)}, /*index=5*/s32[]{:T(128)}, s32[1]{0:T(128)}, s32[]{:T(128)}, s32[1]{0:T(128)}) while((s32[]{:T(128)}, f32[128,256]{1,0:T(8,128)S(1)}, s32[128]{0:T(128)S(1)}, f32[1663,256]{1,0:T(8,128)S(1)}, ...), condition=%wide.region_6.7_spmd, body=%wide.region_4.6_spmd.sunk | while | flops 786182 | bytes 3148967 | solution.py:44
  1259.5 126.4 %all-reduce.4.cloned.1.call-done = f32[512,128]{1,0:T(8,128)} async-done(((f32[512,128]{1,0:T(8,128)}), f32[512,128]{1,0:T(8,128)}) %all-reduce.4.cloned.1.call-update) | async-done | bytes 262160 | tf_op jit(solution)/shard_map/psum | solution.py:95
  (918 shorter events, 722.9 us)
Async XLA Ops:
  7.2 252.6 %copy-start = (f32[512,128]{1,0:T(8,128)S(1)}, f32[512,128]{1,0:T(8,128)}, u32[]{:S(2)}) copy-start(f32[512,128]{1,0:T(8,128)} %param.17) | copy-start | bytes 786436
  7.2 68.6 %all-gather.3.cloned.1.call-start = ((), (), s32[]{:S(2)}) async-start(), calls=%async_computation.4 | async-start | bytes 3932160 | tf_op jit(solution)/shard_map/all_gather | solution.py:65
  7.9 229.3 %copy-start.7 = (bf16[192,2048]{1,0:T(8,128)(2,1)S(1)}, bf16[192,2048]{1,0:T(8,128)(2,1)}, u32[]{:S(2)}) copy-start(bf16[192,2048]{1,0:T(8,128)(2,1)} %param.14) | copy-start | bytes 2359300
  7.9 229.3 %all-gather.5.cloned.1.call-start = ((), (), s32[]{:S(2)}) async-start(), calls=%async_computation.5 | async-start | bytes 37748736 | tf_op jit(solution)/shard_map/all_gather | solution.py:64
  256.1 16.1 %all-to-all-start.2 = ((bf16[192,8,256]{2,0,1:T(8,128)(2,1)}), bf16[192,8,256]{2,0,1:T(8,128)(2,1)S(1)}, u32[]{:S(2)}, u32[]{:S(2)}) async-start(bf16[192,8,256]{2,0,1:T(8,128)(2,1)} %bitcast.31), calls=%async_computation.2 | async-start | bytes 1572864 | tf_op jit(solution)/shard_map/all_to_all | solution.py:71
  272.4 2.0 copy-start.2
  580.4 1.1 copy-start.5
  580.4 1.4 copy-start.6
  584.3 16.1 %all-to-all-start = ((bf16[192,8,256]{2,0,1:T(8,128)(2,1)}), bf16[192,8,256]{2,0,1:T(8,128)(2,1)S(1)}, u32[]{:S(2)}, u32[]{:S(2)}) async-start(bf16[192,8,256]{2,0,1:T(8,128)(2,1)} %bitcast.32), calls=%async_computation | async-start | bytes 1572864 | tf_op jit(solution)/shard_map/all_to_all | solution.py:70
  600.4 0.9 copy-start.3
  966.7 420.9 %all-to-all-start.1 = ((f32[8,192,256]{2,1,0:T(8,128)}), f32[8,192,256]{2,1,0:T(8,128)}, u32[]{:S(2)}, u32[]{:S(2)}) async-start(f32[8,192,256]{2,1,0:T(8,128)} %bitcast.46), calls=%async_computation.1 | async-start | bytes 3145728 | tf_op jit(solution)/shard_map/all_to_all | solution.py:87
  970.9 414.9 %all-reduce.4.cloned.1.call-start = ((), (), s32[]{:S(2)}) async-start(), calls=%async_computation.6 | async-start | bytes 524288 | tf_op jit(solution)/shard_map/psum | solution.py:95
  1387.5 1.9 copy-start.4
  1389.2 1.3 copy-start.1
Sparse Core Ops, SparseCore 0:
  9.6 66.1 all-gather.2
  77.7 159.4 all-gather.4
  1259.6 126.2 all-reduce.3
where the time goes:
time: 1410 us; the launch traced here: 1400 us
  other arithmetic  685 us (49%)
  waiting for transfers between devices  381 us (27%)
  loops' own time  173 us (12%)
  local copies, waits for them, and re-layouts  89.3 us (6%)
  blocking collectives  23.4 us (2%)
  matrix products  19.7 us (1%)
    add x128, other arithmetic, causal_step(): return total + weight * window  363 us
    add x128, other arithmetic, anticausal_step(): return total + weight * window  278 us
    another operation x1, loops' own time, lagged(): return lax.map(one_lag, jnp.arange(prev + 1, dtype=jnp.int32))  169 us
    all_gather x1, waiting for transfers between devices, body(): panel = lax.all_gather(out_weight, 'ctx', axis=1, tiled=True)  161 us
    psum x1, waiting for transfers between devices, body(): grad_filters = lax.psum(partial_terms, ('ctx', 'mp')) * scale  126 us
    dynamic_slice x128, local copies, waits for them, and re-layouts, lagged(): return lax.map(one_lag, jnp.arange(prev + 1, dtype=jnp.int32))  75 us
    all_gather x1, waiting for transfers between devices, body(): lax.all_gather(cotangent, 'mp', axis=1, tiled=True)  67.1 us
    reduce_sum x128, other arithmetic, one_lag(): return jnp.sum(window * gradient, axis=0)  38.9 us
  transfers between devices with their start and end apart: 6, of which 5 were waited for; matrix products, arithmetic and copies ran while one was open for 9% of the time, Pallas kernels for 0%

commit v1 on v0

--- a/solution.py
+++ b/solution.py
@@ -1,7 +1,29 @@
+import functools
 import jax
 import jax.numpy as jnp
 from jax import lax
 from jax.sharding import PartitionSpec as P
+
+
+def enter_cube_in(v0, link_axis):
+    res = jax.lax.axis_size(link_axis)
+    finding, r2 = (res, jax.lax.axis_index(link_axis))
+    plain, y_new = (v0, 1)
+    while y_new < finding:
+        series = []
+        k = 0
+        while k < finding:
+            series.append((k, k ^ y_new))
+            k = k + 1
+        u_next = jax.lax.ppermute(plain, link_axis, perm=series)
+        h_now = jnp.concatenate([plain, u_next], 1)
+        near = jnp.concatenate([u_next, plain], 1)
+        plain = jnp.where(r2 & y_new == 0, h_now, near)
+        y_new = 2 * y_new
+    return plain
+
+
+lift_skins = functools.partial(enter_cube_in, link_axis="mp")
 
 
 def causal(widened, taps, rows, prev):
@@ -62,7 +84,7 @@
     ctx_count = lax.axis_size("ctx")
     per_group = chans * lax.axis_size("mp") // groups
     panel = lax.all_gather(out_weight, "ctx", axis=1, tiled=True)
-    grad_mixed = contract(lax.all_gather(cotangent, "mp", axis=1, tiled=True), panel)
+    grad_mixed = contract(lift_skins(cotangent), panel)
     product = (key_act.astype(jnp.float32) * value_act.astype(jnp.float32)).astype(jnp.bfloat16)
     grad_conv = (grad_mixed * query_act.astype(jnp.float32)).astype(jnp.bfloat16)
     narrow = chans // ctx_count

time: 1410 us -> 1340 us (0.950)
  waiting for transfers between devices: 381 us -> 309 us
    all_gather x1, waiting for transfers between devices: 161 us -> 71.9 us  [body(): panel = lax.all_gather(out_weight, 'ctx', axis=1, tiled=True)]
    ppermute x0 -> x2, waiting for transfers between devices: none -> 85.4 us  [enter_cube_in(): u_next = jax.lax.ppermute(plain, link_axis, perm=series)]
    all_gather x1 -> x0, waiting for transfers between devices: 67.1 us -> none  [body(): lax.all_gather(cotangent, 'mp', axis=1, tiled=True)]
  transfers between devices with their start and end apart: 6 -> 7, of which waited for: 5 -> 6; matrix products, arithmetic and copies ran while one was open for 9% -> 9% of each run, Pallas kernels for 0% -> 0%
where the time goes in v1:
time: 1340 us; the launch traced here: 1330 us
  other arithmetic  686 us (51%)
  waiting for transfers between devices  309 us (23%)
  loops' own time  173 us (13%)
  local copies, waits for them, and re-layouts  89.7 us (7%)
  blocking collectives  23.4 us (2%)
  matrix products  19.6 us (1%)
  starting transfers between devices  17.3 us (1%)
  between operations  14.2 us (1%)
    add x128, other arithmetic, causal_step(): return total + weight * window  362 us
    add x128, other arithmetic, anticausal_step(): return total + weight * window  277 us
    another operation x1, loops' own time, lagged(): return lax.map(one_lag, jnp.arange(prev + 1, dtype=jnp.int32))  169 us
    psum x1, waiting for transfers between devices, body(): grad_filters = lax.psum(partial_terms, ('ctx', 'mp')) * scale  126 us
    ppermute x2, waiting for transfers between devices, enter_cube_in(): u_next = jax.lax.ppermute(plain, link_axis, perm=series)  85.4 us
    dynamic_slice x128, local copies, waits for them, and re-layouts, lagged(): return lax.map(one_lag, jnp.arange(prev + 1, dtype=jnp.int32))  75 us
    all_gather x1, waiting for transfers between devices, body(): panel = lax.all_gather(out_weight, 'ctx', axis=1, tiled=True)  71.9 us
    reduce_sum x128, other arithmetic, one_lag(): return jnp.sum(window * gradient, axis=0)  38.9 us
  transfers between devices with their start and end apart: 7, of which 6 were waited for; matrix products, arithmetic and copies ran while one was open for 9% of the time, Pallas kernels for 0%

profile of v1, /device:TPU:0, one launch (start us, length us, event | category | flops | bytes accessed | tf_op | source)
XLA Modules:
  0.0 1332.3 jit_solution(13944290633413235744)
XLA Ops:
  8.4 3.0 collective-permute-start
  11.4 17.6 %collective-permute-done = bf16[192,2048]{1,0:T(8,128)(2,1)} collective-permute-done((bf16[192,2048]{1,0:T(8,128)(2,1)S(1)}, bf16[192,2048]{1,0:T(8,128)(2,1)}, u32[]{:S(2)}, u32[]{:S(2)}) %collective-permute-start) | collective-permute-done | bytes 786464 | tf_op jit(solution)/shard_map/ppermute | solution.py:18
  33.8 67.8 %collective-permute-done.1 = bf16[192,4096]{1,0:T(8,128)(2,1)} collective-permute-done((bf16[192,4096]{1,0:T(8,128)(2,1)S(1)}, bf16[192,4096]{1,0:T(8,128)(2,1)}, u32[]{:S(2)}, u32[]{:S(2)}) %collective-permute-start.1) | collective-permute-done | bytes 1572896 | tf_op jit(solution)/shard_map/ppermute | solution.py:18
  101.6 71.9 %all-gather.2.cloned.1.call-done = bf16[2048,8192]{1,0:T(8,128)(2,1)} async-done(((bf16[2048,1024]{1,0:T(8,128)(2,1)}), bf16[2048,8192]{1,0:T(8,128)(2,1)}) %all-gather.2.cloned.1.call-update) | async-done | bytes 33554448 | tf_op jit(solution)/shard_map/all_gather | solution.py:86
  173.5 17.9 %multiply_convert_fusion = (bf16[192,2048]{1,0:T(8,128)(2,1)S(1)}, f32[192,2048]{1,0:T(8,128)}) fusion(bf16[192,2048]{1,0:T(8,128)(2,1)} %param.14, bf16[2048,8192]{1,0:T(8,128)(2,1)} %all-gather.2.cloned.1.call-done, bf16[192,4096]{1,0:T(8,128)(2,1)} %collective-permute-done.1, bf16[192,4096]{1,0:T(8,128)(2,1)S(1)} %maximum_select_fusion.2, pred[]{:T(512)S(6)} %eq.19), kind=kOutput, calls=%fused_computation.20 | convolution fusion | flops 6457786368 | bytes 39845888 | tf_op jit(solution)/shard_map/dot_general | solution.py:70
  192.3 3.5 all-to-all-start.2
  196.6 11.8 all-to-all-done.2
  210.5 282.3 %while.38 = (s32[]{:T(128)}, f32[1536,256]{1,0:T(8,128)S(1)}, f32[128,256]{1,0:T(8,128)S(1)}, f32[1663,256]{1,0:T(8,128)}, s32[]{:T(128)}, /*index=5*/s32[]{:T(128)}) while((s32[]{:T(128)}, f32[1536,256]{1,0:T(8,128)S(1)}, f32[128,256]{1,0:T(8,128)S(1)}, f32[1663,256]{1,0:T(8,128)}, s32[]{:T(128)}, /*index=5*/s32[]{:T(128)}) %tuple.96), condition=%wide.region_3.4_spmd.clone, body=%wide.region_2.3_spmd.clone.sunk | while | flops 1179651 | bytes 4721751 | solution.py:51
  492.8 23.4 %all_to_all.64 = f32[8,192,256]{2,1,0:T(8,128)S(1)} all-to-all(f32[8,192,256]{2,1,0:T(8,128)S(1)} %bitcast.44), channel_id=1, replica_groups=mesh['ctx'=8,'mp'=4] {'ctx'}, dimensions={0} | all-to-all | bytes 3145728 | tf_op jit(solution)/shard_map/all_to_all | solution.py:110
  520.2 3.5 all-to-all-start
  523.7 12.5 all-to-all-done
  538.4 363.2 %while.37 = (s32[]{:T(128)}, f32[1536,256]{1,0:T(8,128)}, f32[128,256]{1,0:T(8,128)S(1)}, f32[1663,256]{1,0:T(8,128)S(1)}, s32[]{:T(128)}, /*index=5*/s32[]{:T(128)}, s32[]{:T(128)}, s32[]{:T(128)}) while((s32[]{:T(128)}, f32[1536,256]{1,0:T(8,128)}, f32[128,256]{1,0:T(8,128)S(1)}, f32[1663,256]{1,0:T(8,128)S(1)}, s32[]{:T(128)}, ...), condition=%wide.region_1.2_spmd.clone, body=%wide.region_0.1_spmd.clone.sunk | while | flops 1179655 | bytes 4721813 | solution.py:36
  540.0 2.9 select_add_fusion.4
  548.6 2.9 select_add_fusion.4
  554.4 2.9 select_add_fusion.4
  557.3 2.9 select_add_fusion.4
  582.6 2.9 select_add_fusion.4
  588.4 2.9 select_add_fusion.4
  597.1 2.9 select_add_fusion.4
  602.9 2.9 select_add_fusion.4
  628.2 2.9 select_add_fusion.4
  636.9 2.9 select_add_fusion.4
  642.7 2.9 select_add_fusion.4
  645.6 2.9 select_add_fusion.4
  676.7 2.9 select_add_fusion.4
  685.3 2.9 select_add_fusion.4
  691.1 2.9 select_add_fusion.4
  694.0 2.9 select_add_fusion.4
  725.1 2.9 select_add_fusion.4
  901.6 4.3 all-to-all-start.1
  906.0 287.3 %while.36 = (s32[]{:T(128)}, f32[128,256]{1,0:T(8,128)S(1)}, s32[128]{0:T(128)S(1)}, f32[1663,256]{1,0:T(8,128)S(1)}, f32[1536,256]{1,0:T(8,128)S(1)}, /*index=5*/s32[]{:T(128)}, s32[1]{0:T(128)}, s32[]{:T(128)}, s32[1]{0:T(128)}) while((s32[]{:T(128)}, f32[128,256]{1,0:T(8,128)S(1)}, s32[128]{0:T(128)S(1)}, f32[1663,256]{1,0:T(8,128)S(1)}, ...), condition=%wide.region_6.7_spmd, body=%wide.region_4.6_spmd.sunk | while | flops 786182 | bytes 3148959 | solution.py:66
  1194.4 126.4 %all-reduce.4.cloned.1.call-done = f32[512,128]{1,0:T(8,128)} async-done(((f32[512,128]{1,0:T(8,128)}), f32[512,128]{1,0:T(8,128)}) %all-reduce.4.cloned.1.call-update) | async-done | bytes 262160 | tf_op jit(solution)/shard_map/psum | solution.py:117
  (920 shorter events, 732.1 us)
Async XLA Ops:
  7.2 188.7 %copy-start = (f32[512,128]{1,0:T(8,128)S(1)}, f32[512,128]{1,0:T(8,128)}, u32[]{:S(2)}) copy-start(f32[512,128]{1,0:T(8,128)} %param.17) | copy-start | bytes 786436
  7.2 1.2 copy-start.5
  7.2 166.3 %all-gather.2.cloned.1.call-start = ((), (), s32[]{:S(2)}) async-start(), calls=%async_computation.4 | async-start | bytes 37748736 | tf_op jit(solution)/shard_map/all_gather | solution.py:86
  8.4 20.7 %collective-permute-start = (bf16[192,2048]{1,0:T(8,128)(2,1)S(1)}, bf16[192,2048]{1,0:T(8,128)(2,1)}, u32[]{:S(2)}, u32[]{:S(2)}) collective-permute-start(bf16[192,2048]{1,0:T(8,128)(2,1)S(1)} %copy-done.5), channel_id=1, source_target_pairs={{0,1},{1,0},{2,3},{3,2},{4,5},{5,4},{6,7},{7,6},{8,9},{9,8},{10,11... | collective-permute-start | bytes 2359304 | tf_op jit(solution)/shard_map/ppermute | solution.py:18
  31.0 70.6 %collective-permute-start.1 = (bf16[192,4096]{1,0:T(8,128)(2,1)S(1)}, bf16[192,4096]{1,0:T(8,128)(2,1)}, u32[]{:S(2)}, u32[]{:S(2)}) collective-permute-start(bf16[192,4096]{1,0:T(8,128)(2,1)S(1)} %maximum_select_fusion.2), channel_id=1, source_target_pairs={{0,2},{1,3},{2,0},{3,1},{4,6},{5,7},{6,4},{7,5},{8,10},{9,11},{10,... | collective-permute-start | bytes 4718600 | tf_op jit(solution)/shard_map/ppermute | solution.py:18
  192.3 16.1 %all-to-all-start.2 = ((bf16[192,8,256]{2,0,1:T(8,128)(2,1)}), bf16[192,8,256]{2,0,1:T(8,128)(2,1)S(1)}, u32[]{:S(2)}, u32[]{:S(2)}) async-start(bf16[192,8,256]{2,0,1:T(8,128)(2,1)} %bitcast.30), calls=%async_computation.2 | async-start | bytes 1572864 | tf_op jit(solution)/shard_map/all_to_all | solution.py:93
  208.5 2.0 copy-start.2
  516.2 1.1 copy-start.6
  516.2 1.4 copy-start.7
  520.2 16.1 %all-to-all-start = ((bf16[192,8,256]{2,0,1:T(8,128)(2,1)}), bf16[192,8,256]{2,0,1:T(8,128)(2,1)S(1)}, u32[]{:S(2)}, u32[]{:S(2)}) async-start(bf16[192,8,256]{2,0,1:T(8,128)(2,1)} %bitcast.31), calls=%async_computation | async-start | bytes 1572864 | tf_op jit(solution)/shard_map/all_to_all | solution.py:92
  536.3 0.9 copy-start.3
  901.6 420.9 %all-to-all-start.1 = ((f32[8,192,256]{2,1,0:T(8,128)}), f32[8,192,256]{2,1,0:T(8,128)}, u32[]{:S(2)}, u32[]{:S(2)}) async-start(f32[8,192,256]{2,1,0:T(8,128)} %bitcast.45), calls=%async_computation.1 | async-start | bytes 3145728 | tf_op jit(solution)/shard_map/all_to_all | solution.py:109
  905.9 414.9 %all-reduce.4.cloned.1.call-start = ((), (), s32[]{:S(2)}) async-start(), calls=%async_computation.5 | async-start | bytes 524288 | tf_op jit(solution)/shard_map/psum | solution.py:117
  1322.5 1.9 copy-start.4
  1324.2 1.3 copy-start.1
Sparse Core Ops, SparseCore 0:
  9.9 163.4 all-gather.1
  1194.5 126.2 all-reduce.3
